TPU v7x, 32 devices: a whole 2x2x4 slice. The times are simulated.
32 devices in a mesh: seq: 8 (over z, y), fsdp: 4 (over x, core).
Axes of the slice: x: 2, y: 2, z: 4, core: 2. Of those that a mesh axis runs over, the one named last changes fastest.
Arguments:
- inputs: bfloat16 [12288, 1536], P(('seq', 'fsdp')), may hold values from -15 to 15
- layer_norm_gain: float32 [1536], replicated, may hold values from 0.25 to 1.75
- layer_norm_bias: float32 [1536], replicated, may hold values from -4 to 4
- w_in: bfloat16 [1536, 3072], P('fsdp'), may hold values from -0.15625 to 0.15625
- dw_kernel: float32 [32, 1536], replicated, may hold values from -1 to 1
- bn_gain: float32 [1536], replicated, may hold values from 0.25 to 1.75
- bn_bias: float32 [1536], replicated, may hold values from -4 to 4
- cotangent: bfloat16 [12288, 1536], P(('seq', 'fsdp')), may hold values from -6 to 6
Outputs:
- output: bfloat16 [12288, 1536], P(('seq', 'fsdp'))
- input_gradient: bfloat16 [12288, 1536], P(('seq', 'fsdp'))
- grad_w_in: float32 [1536, 3072], P('fsdp')
- grad_kernel: float32 [32, 1536], replicated
- grad_bn_gain: float32 [1536], replicated
- grad_bn_bias: float32 [1536], replicated
- layer_norm_gain_gradient: float32 [1536], replicated
- grad_ln_bias: float32 [1536], replicated
All inputs are finite; a program needn't handle non-finite values.
Results may differ from a plain program's by a relative error of at most 0.012.
The roundings to bfloat16 on the way count: a program that leaves them out, or rounds other values in their place, can miss the bound.
Values may be sent and summed in bfloat16 or wider, within the bound.
No kernel may reach another device: no remote copies, remote signals or barrier semaphores. Data moves between devices by JAX's collectives and lax.ppermute only.
A program may use at most 128 MiB of HBM per device.

v0:
```python
import jax
import jax.numpy as jnp
from jax import lax
from jax.sharding import PartitionSpec as P

epsilon = 1e-05


def from_behind(block, axis, distance):
    devices = range(lax.axis_size(axis))
    route = [(i - distance, i) for i in devices if i - distance in devices]
    return lax.ppermute(block, axis, route)


def tree_sum(tree, axis):
    count = lax.axis_size(axis)
    if count & count - 1:
        return lax.psum(tree, axis)
    stride = 1
    while stride < count:
        route = [(i, i ^ stride) for i in range(count)]
        tree = jax.tree.map(lambda x: x + lax.ppermute(x, axis, route), tree)
        stride *= 2
    return tree


def on_device(
    inputs, layer_norm_gain, layer_norm_bias, w_in, dw_kernel, bn_gain, bn_bias, cotangent
):
    tok_rows = inputs.shape[0]
    features = inputs.shape[1]
    kernel_len = dw_kernel.shape[0]
    all_frames = tok_rows * lax.axis_size("seq") * lax.axis_size("fsdp")
    frames = inputs.astype(jnp.float32)
    row_mean = jnp.mean(frames, axis=-1, keepdims=True)
    centered_rows = frames - row_mean
    row_inverse_deviation = lax.rsqrt(
        jnp.mean(centered_rows * centered_rows, axis=-1, keepdims=True) + epsilon
    )
    standardized_input = centered_rows * row_inverse_deviation
    normalized_rows = (standardized_input * layer_norm_gain + layer_norm_bias).astype(jnp.bfloat16)
    full_weight = lax.all_gather(w_in, "fsdp", axis=0, tiled=True)
    hidden = jnp.dot(normalized_rows, full_weight, preferred_element_type=jnp.float32)
    value_part = hidden[:, :features]
    gate_sig = jax.nn.sigmoid(hidden[:, features:])
    glu = (value_part * gate_sig).astype(jnp.bfloat16)
    past_rim = from_behind(glu[tok_rows - (kernel_len - 1) :], ("seq", "fsdp"), 1)
    padded_glu = jnp.concatenate([past_rim, glu], axis=0).astype(jnp.float32)
    conv_out = jnp.zeros((tok_rows, features), jnp.float32)
    for offset in range(kernel_len):
        conv_out = (
            conv_out
            + dw_kernel[offset]
            * padded_glu[kernel_len - 1 - offset : kernel_len - 1 - offset + tok_rows]
        )
    chan_mean = tree_sum(jnp.sum(conv_out, axis=0), ("seq", "fsdp")) / all_frames
    conv_centred = conv_out - chan_mean
    chan_var = tree_sum(jnp.sum(conv_centred * conv_centred, axis=0), ("seq", "fsdp")) / all_frames
    bn_rstd = lax.rsqrt(chan_var + epsilon)
    chat = conv_centred * bn_rstd
    z_value = chat * bn_gain + bn_bias
    z_sig = jax.nn.sigmoid(z_value)
    output = (z_value * z_sig).astype(jnp.bfloat16)
    grad_z = cotangent.astype(jnp.float32) * z_sig * (1.0 + z_value * (1.0 - z_sig))
    grad_bn_bias, grad_bn_gain = tree_sum(
        (jnp.sum(grad_z, axis=0), jnp.sum(grad_z * chat, axis=0)), ("seq", "fsdp")
    )
    grad_conv = (
        bn_gain * bn_rstd * (grad_z - grad_bn_bias / all_frames - chat * grad_bn_gain / all_frames)
    )
    future_rim = from_behind(grad_conv[: kernel_len - 1], ("seq", "fsdp"), -1)
    padded_grad = jnp.concatenate([grad_conv, future_rim], axis=0)
    grad_glu = jnp.zeros((tok_rows, features), jnp.float32)
    kernel_rows = []
    for offset in range(kernel_len):
        grad_glu = grad_glu + dw_kernel[offset] * padded_grad[offset : offset + tok_rows]
        kernel_rows.append(
            jnp.sum(
                grad_conv
                * padded_glu[kernel_len - 1 - offset : kernel_len - 1 - offset + tok_rows],
                axis=0,
            )
        )
    kernel_portion = jnp.stack(kernel_rows, axis=0)
    grad_value = grad_glu * gate_sig
    grad_gate = grad_glu * value_part * gate_sig * (1.0 - gate_sig)
    grad_hidden = jnp.concatenate([grad_value, grad_gate], axis=1).astype(jnp.bfloat16)
    normalized_gradient = lax.dot_general(
        grad_hidden, full_weight, (((1,), (1,)), ((), ())), preferred_element_type=jnp.float32
    )
    grad_kernel, layer_norm_gain_gradient, grad_ln_bias = tree_sum(
        (
            kernel_portion,
            jnp.sum(normalized_gradient * standardized_input, axis=0),
            jnp.sum(normalized_gradient, axis=0),
        ),
        ("seq", "fsdp"),
    )
    rescaled_rows = normalized_gradient * layer_norm_gain
    input_gradient = row_inverse_deviation * (
        rescaled_rows
        - jnp.mean(rescaled_rows, axis=-1, keepdims=True)
        - standardized_input * jnp.mean(rescaled_rows * standardized_input, axis=-1, keepdims=True)
    )
    row_share = lax.psum_scatter(
        lax.dot_general(
            normalized_rows,
            grad_hidden,
            (((0,), (0,)), ((), ())),
            preferred_element_type=jnp.float32,
        ),
        "fsdp",
        scatter_dimension=0,
        tiled=True,
    )
    grad_w_in = lax.psum(row_share, "seq")
    return (
        output,
        input_gradient.astype(jnp.bfloat16),
        grad_w_in,
        grad_kernel,
        grad_bn_gain,
        grad_bn_bias,
        layer_norm_gain_gradient,
        grad_ln_bias,
    )


def solution(mesh):
    placed = (
        P(("seq", "fsdp"), None),
        P(),
        P(),
        P("fsdp", None),
        P(),
        P(),
        P(),
        P(("seq", "fsdp"), None),
    )
    return jax.shard_map(
        on_device,
        mesh=mesh,
        in_specs=placed,
        out_specs=(
            P(("seq", "fsdp"), None),
            P(("seq", "fsdp"), None),
            P("fsdp", None),
            P(),
            P(),
            P(),
            P(),
            P(),
        ),
        check_vma=False,
    )
```

profile of v0, /device:TPU:0, one launch (start us, length us, event | category | flops | bytes accessed | tf_op | source)
XLA Modules:
  0.0 560.9 jit_solution(14859436354774125420)
XLA Ops:
  9.3 67.3 %all-gather.2.cloned.1.call-done = bf16[1536,3072]{1,0:T(8,128)(2,1)} async-done(((bf16[384,3072]{1,0:T(8,128)(2,1)}), bf16[1536,3072]{1,0:T(8,128)(2,1)}) %all-gather.2.cloned.1.call-update) | async-done | bytes 9437200 | tf_op jit(solution)/shard_map/all_gather | solution.py:42
  76.6 6.7 %fusion.114 = f32[384,3072]{1,0:T(8,128)S(1)} fusion(bf16[1536,3072]{1,0:T(8,128)(2,1)} %all-gather.2.cloned.1.call-done, bf16[384,1536]{1,0:T(8,128)(2,1)S(1)} %copy-done.2, f32[1536]{0:T(1024)S(1)} %copy-done.10, f32[1536]{0:T(1024)S(1)} %copy-done.9, f32[384]{0:T(512)S(1)} %add_rsqrt_fusion.1, f32[384]{0:T(512)S(1)} %broadcast_multiply_fusion.3), kind=kOutput, calls=%fused_computation.258 | convolution fusion | flops 3627417600 | bytes 15350784 | tf_op jit(solution)/shard_map/dot_general | solution.py:43
  83.9 1.5 copy-done
  85.5 2.2 collective-permute-start
  88.9 9.4 %fusion.119 = (f32[1536]{0:T(1024)S(1)}, f32[384,1536]{1,0:T(8,128)S(1)}) fusion(f32[415,1536]{1,0:T(8,128)S(1)} %maximum_convert_fusion, f32[1536]{0:T(1024)S(1)} %get-tuple-element.76, f32[1536]{0:T(1024)S(1)} %get-tuple-element.77, f32[1536]{0:T(1024)S(1)} %get-tuple-element.47, f32[1536]{0:T(1024)S(1)} %get-tuple-element.48, ...), kind=kLoop, calls=%fused_computation.261 | loop fusion | flops 37747200 | bytes 78059520 | tf_op jit(solution)/shard_map/reduce_sum | solution.py:56
  100.2 2.6 collective-permute-start.2
  102.8 1.6 collective-permute-done.2
  104.4 4.1 collective-permute-start.3
  108.5 1.6 collective-permute-done.3
  110.2 2.9 collective-permute-start.4
  113.1 1.6 collective-permute-done.4
  114.7 2.9 collective-permute-start.5
  117.7 1.6 collective-permute-done.5
  120.8 3.6 collective-permute-done.7
  125.6 2.6 collective-permute-done.8
  128.1 2.0 collective-permute-start.9
  130.1 1.6 collective-permute-done.9
  131.8 2.9 collective-permute-start.10
  134.7 1.6 collective-permute-done.10
  136.4 2.5 fusion.116
  140.2 1.9 collective-permute-start.17
  142.1 1.6 collective-permute-done.12
  145.7 1.6 collective-permute-done.13
  147.4 2.0 collective-permute-start.14
  151.0 2.9 collective-permute-start.15
  153.9 1.6 collective-permute-start.20
  156.2 2.3 collective-permute-done.20
  158.5 7.1 %multiply_reduce_fusion = (f32[1536]{0:T(1024)S(1)}, f32[1536]{0:T(1024)S(1)}, f32[1536]{0:T(1024)S(1)}, f32[1536]{0:T(1024)S(1)}, f32[1536]{0:T(1024)S(1)}, /*i...) fusion(f32[415,1536]{1,0:T(8,128)S(1)} %maximum_convert_fusion,, ...), kind=kLoop, calls=%fused_computation.169 | loop fusion | flops 31822848 | bytes 48519168 | tf_op jit(solution)/shard_map/reduce_sum | solution.py:78
  168.5 1.9 collective-permute-done.21
  170.3 40.4 %multiply_convert_fusion.1 = (bf16[384,1536]{1,0:T(8,128)(2,1)S(1)}, f32[384,1536]{1,0:T(8,128)}) fusion(f32[384,3072]{1,0:T(8,128)} %copy-done, f32[31,1536]{1,0:T(8,128)S(1)} %collective-permute-done.21, f32[384,1536]{1,0:T(8,128)} %copy-done.1, f32[1536]{0:T(1024)S(1)} %get-tuple-element.76, f32[1536]{0:T(1024)S(1)} %get-tuple-element.77, ...), kind=kLoop, calls=%fused_computation.202 | loop fusion | flops 58392576 | bytes 8644608 | tf_op jit(solution)/shard_map/convert
  210.8 4.4 multiply_convert_fusion
  216.3 9.4 %fusion.109 = f32[1536,3072]{1,0:T(8,128)} fusion(bf16[384,1536]{1,0:T(8,128)(2,1)S(1)} %multiply_convert_fusion, bf16[384,1536]{1,0:T(8,128)(2,1)S(1)} %get-tuple-element.79, bf16[384,1536]{1,0:T(8,128)(2,1)S(1)} %copy-done.3, f32[1536]{0:T(1024)S(1)} %copy-done.10, f32[1536]{0:T(1024)S(1)} %copy-done.9, f32[384]{0:T(512)S(1)} %add_rsqrt_fusion.1, ...), kind=kOutput, calls=%fused_computation.214 | convolution fusion | flops 3632136192 | bytes 22428672 | tf_op jit(solution)/shard_map/dot_general | solution.py:106
  226.0 140.8 %reduce-scatter.2.cloned.1.call-done = f32[384,3072]{1,0:T(8,128)} async-done(((f32[1536,3072]{1,0:T(8,128)}), f32[384,3072]{1,0:T(8,128)}) %reduce-scatter.2.cloned.1.call-update) | async-done | bytes 4718608 | tf_op jit(solution)/shard_map/reduce_scatter | solution.py:105
  366.8 5.4 multiply_reduce_fusion.18
  374.9 6.6 %collective-permute-done.23 = f32[32,1536]{1,0:T(8,128)S(1)} collective-permute-done((f32[32,1536]{1,0:T(8,128)S(1)}, f32[32,1536]{1,0:T(8,128)S(1)}, u32[]{:S(2)}, u32[]{:S(2)}) %collective-permute-start.23) | collective-permute-done | bytes 196640 | tf_op jit(solution)/shard_map/ppermute | solution.py:22
  381.6 1.5 collective-permute-start.24
  383.1 9.1 %fusion.12 = (f32[1536]{0:T(1024)S(1)}, f32[384]{0:T(512)S(1)}, f32[384]{0:T(512)S(1)}, f32[1536]{0:T(1024)S(1)}, f32[384,1536]{1,0:T(8,128)S(1)}) fusion(bf16[384,1536]{1,0:T(8,128)(2,1)} %param.8, f32[384]{0:T(512)S(1)} %add_rsqrt_fusion.1, f32[384]{0:T(512)S(1)} %broadcast_multiply_fusion.3, f32[1536]{0:T(1024)S(1)} %copy-done.9, ...), kind=kOutput, calls=%fused_computation.44 | convolution fusion | flops 3634491392 | bytes 15360000 | tf_op jit(solution)/shard_map/dot_general | solution.py:88
  395.5 1.6 collective-permute-done.28
  399.2 1.6 collective-permute-done.29
  400.8 1.5 collective-permute-start.30
  402.9 1.5 collective-permute-start.25
  404.4 2.2 collective-permute-done.30
  407.1 2.4 collective-permute-start.36
  409.5 17.2 %collective-permute-done.25 = f32[32,1536]{1,0:T(8,128)S(1)} collective-permute-done((f32[32,1536]{1,0:T(8,128)S(1)}, f32[32,1536]{1,0:T(8,128)S(1)}, u32[]{:S(2)}, u32[]{:S(2)}) %collective-permute-start.25) | collective-permute-done | bytes 196640 | tf_op jit(solution)/shard_map/ppermute | solution.py:22
  427.3 1.8 fusion.11
  430.3 9.8 %collective-permute-done.26 = f32[32,1536]{1,0:T(8,128)S(1)} collective-permute-done((f32[32,1536]{1,0:T(8,128)S(1)}, f32[32,1536]{1,0:T(8,128)S(1)}, u32[]{:S(2)}, u32[]{:S(2)}) %collective-permute-start.26) | collective-permute-done | bytes 196640 | tf_op jit(solution)/shard_map/ppermute | solution.py:22
  440.8 108.5 %all-reduce.2.cloned.1.call-done = f32[384,3072]{1,0:T(8,128)} async-done(((f32[384,3072]{1,0:T(8,128)}), f32[384,3072]{1,0:T(8,128)}) %all-reduce.2.cloned.1.call-update) | async-done | bytes 4718608 | tf_op jit(solution)/shard_map/psum | solution.py:116
  549.3 5.1 copy.17
  (154 shorter events, 29.6 us)
Async XLA Ops:
  7.2 69.4 %copy-start.9 = (f32[1536]{0:T(1024)S(1)}, f32[1536]{0:T(1024)}, u32[]{:S(2)}) copy-start(f32[1536]{0:T(1024)} %param.9) | copy-start | bytes 18436
  7.2 69.4 %copy-start.10 = (f32[1536]{0:T(1024)S(1)}, f32[1536]{0:T(1024)}, u32[]{:S(2)}) copy-start(f32[1536]{0:T(1024)} %param.10) | copy-start | bytes 18436
  7.2 69.4 %all-gather.2.cloned.1.call-start = ((), (), s32[]{:S(2)}) async-start(), calls=%async_computation.1 | async-start | bytes 11796480 | tf_op jit(solution)/shard_map/all_gather | solution.py:42
  7.9 358.8 %reduce-scatter.2.cloned.1.call-start = ((), (), s32[]{:S(2)}) async-start(), calls=%async_computation.2 | async-start | bytes 23592960 | tf_op jit(solution)/shard_map/reduce_scatter | solution.py:105
  85.5 3.1 collective-permute-start
  98.4 38.0 %copy-start.11 = (f32[1536]{0:T(1024)S(1)}, f32[1536]{0:T(1024)}, u32[]{:S(2)}) copy-start(f32[1536]{0:T(1024)} %param.13) | copy-start | bytes 18436
  98.4 38.0 %copy-start.5 = (bf16[384,1536]{1,0:T(8,128)(2,1)S(1)}, bf16[384,1536]{1,0:T(8,128)(2,1)}, u32[]{:S(2)}) copy-start(bf16[384,1536]{1,0:T(8,128)(2,1)} %param.15) | copy-start | bytes 3538948
  98.4 38.0 %copy-start.12 = (f32[1536]{0:T(1024)S(1)}, f32[1536]{0:T(1024)}, u32[]{:S(2)}) copy-start(f32[1536]{0:T(1024)} %param.14) | copy-start | bytes 18436
  98.4 1.8 collective-permute-start.1
  100.2 4.3 collective-permute-start.2
  104.4 5.7 %collective-permute-start.3 = (f32[1536]{0:T(1024)S(1)}, f32[1536]{0:T(1024)S(1)}, u32[]{:S(2)}, u32[]{:S(2)}) collective-permute-start(f32[1536]{0:T(1024)S(1)} %add.374), channel_id=1, source_target_pairs={{0,4},{1,5},{2,6},{3,7},{4,0},{5,1},{6,2},{7,3},{8,12},{9,13},{10,... | collective-permute-start | bytes 18440 | tf_op jit(solution)/shard_map/ppermute | solution.py:22
  110.2 4.6 collective-permute-start.4
  114.7 4.6 collective-permute-start.5
  119.6 1.2 collective-permute-start.6
  120.8 3.7 collective-permute-start.7
  124.5 3.7 collective-permute-start.8
  128.1 3.7 collective-permute-start.9
  131.8 4.6 collective-permute-start.10
  138.9 1.2 collective-permute-start.11
  138.9 1.3 collective-permute-start.16
  140.0 3.7 collective-permute-start.12
  140.2 4.6 collective-permute-start.17
  143.7 3.7 collective-permute-start.13
  144.8 4.6 collective-permute-start.18
  147.4 3.7 collective-permute-start.14
  149.4 4.6 collective-permute-start.19
  151.0 4.5 collective-permute-start.15
  153.9 4.6 collective-permute-start.20
  158.5 7.1 %copy-start.13 = (f32[1536]{0:T(1024)}, f32[1536]{0:T(1024)S(1)}, u32[]{:S(2)}) copy-start(f32[1536]{0:T(1024)S(1)} %add.398) | copy-start | bytes 18436
  167.0 3.3 collective-permute-start.21
  210.8 5.5 copy-start.3
  225.7 323.6 %all-reduce.2.cloned.1.call-start = ((), (), s32[]{:S(2)}) async-start(), calls=%async_computation.3 | async-start | bytes 9437184 | tf_op jit(solution)/shard_map/psum | solution.py:116
  373.0 1.5 collective-permute-start.22
  374.6 7.0 %collective-permute-start.23 = (f32[32,1536]{1,0:T(8,128)S(1)}, f32[32,1536]{1,0:T(8,128)S(1)}, u32[]{:S(2)}, u32[]{:S(2)}) collective-permute-start(f32[32,1536]{1,0:T(8,128)S(1)} %add.430), channel_id=1, source_target_pairs={{0,2},{1,3},{2,0},{3,1},{4,6},{5,7},{6,4},{7,5},{8,10},{9,11},{10,... | collective-permute-start | bytes 589832 | tf_op jit(solution)/shard_map/ppermute | solution.py:22
  381.6 45.7 %copy-start.4 = (bf16[384,1536]{1,0:T(8,128)(2,1)S(1)}, bf16[384,1536]{1,0:T(8,128)(2,1)}, u32[]{:S(2)}) copy-start(bf16[384,1536]{1,0:T(8,128)(2,1)} %param.8) | copy-start | bytes 3538948
  381.6 21.3 %collective-permute-start.24 = (f32[32,1536]{1,0:T(8,128)S(1)}, f32[32,1536]{1,0:T(8,128)S(1)}, u32[]{:S(2)}, u32[]{:S(2)}) collective-permute-start(f32[32,1536]{1,0:T(8,128)S(1)} %add.431), channel_id=1, source_target_pairs={{0,4},{1,5},{2,6},{3,7},{4,0},{5,1},{6,2},{7,3},{8,12},{9,13},{10,... | collective-permute-start | bytes 589832 | tf_op jit(solution)/shard_map/ppermute | solution.py:22
  392.2 1.2 collective-permute-start.27
  392.3 1.7 collective-permute-start.32
  393.5 3.7 collective-permute-start.28
  394.0 3.7 collective-permute-start.33
  397.1 3.7 collective-permute-start.29
  397.7 4.6 collective-permute-start.34
  400.8 5.8 %collective-permute-start.30 = (f32[1536]{0:T(1024)S(1)}, f32[1536]{0:T(1024)S(1)}, u32[]{:S(2)}, u32[]{:S(2)}) collective-permute-start(f32[1536]{0:T(1024)S(1)} %add.437), channel_id=1, source_target_pairs={{0,8},{1,9},{2,10},{3,11},{4,12},{5,13},{6,14},{7,15},{8,0},{9,1},... | collective-permute-start | bytes 18440 | tf_op jit(solution)/shard_map/ppermute | solution.py:22
  402.3 4.8 collective-permute-start.35
  402.9 23.9 %collective-permute-start.25 = (f32[32,1536]{1,0:T(8,128)S(1)}, f32[32,1536]{1,0:T(8,128)S(1)}, u32[]{:S(2)}, u32[]{:S(2)}) collective-permute-start(f32[32,1536]{1,0:T(8,128)S(1)} %add.432), channel_id=1, source_target_pairs={{0,8},{1,9},{2,10},{3,11},{4,12},{5,13},{6,14},{7,15},{8,0},{9,1},... | collective-permute-start | bytes 589832 | tf_op jit(solution)/shard_map/ppermute | solution.py:22
  406.6 22.5 %collective-permute-start.31 = (f32[1536]{0:T(1024)S(1)}, f32[1536]{0:T(1024)S(1)}, u32[]{:S(2)}, u32[]{:S(2)}) collective-permute-start(f32[1536]{0:T(1024)S(1)} %add.438), channel_id=1, source_target_pairs={{0,16},{1,17},{2,18},{3,19},{4,20},{5,21},{6,22},{7,23},{8,24},{9,... | collective-permute-start | bytes 18440 | tf_op jit(solution)/shard_map/ppermute | solution.py:22
  407.1 22.6 %collective-permute-start.36 = (f32[1536]{0:T(1024)S(1)}, f32[1536]{0:T(1024)S(1)}, u32[]{:S(2)}, u32[]{:S(2)}) collective-permute-start(f32[1536]{0:T(1024)S(1)} %add.443), channel_id=1, source_target_pairs={{0,16},{1,17},{2,18},{3,19},{4,20},{5,21},{6,22},{7,23},{8,24},{9,... | collective-permute-start | bytes 18440 | tf_op jit(solution)/shard_map/ppermute | solution.py:22
  426.8 13.4 %collective-permute-start.26 = (f32[32,1536]{1,0:T(8,128)S(1)}, f32[32,1536]{1,0:T(8,128)S(1)}, u32[]{:S(2)}, u32[]{:S(2)}) collective-permute-start(f32[32,1536]{1,0:T(8,128)S(1)} %add.433), channel_id=1, source_target_pairs={{0,16},{1,17},{2,18},{3,19},{4,20},{5,21},{6,22},{7,23},{8,24},{9,... | collective-permute-start | bytes 589832 | tf_op jit(solution)/shard_map/ppermute | solution.py:22
  (6 other events, 11.4 us)
Sparse Core Ops, SparseCore 0:
  9.6 66.9 all-gather.1
  225.8 140.8 reduce-scatter.1
  370.8 178.4 all-reduce.1
where the time goes:
time: 561 us
  waiting for transfers between devices  387 us (69%)
  other arithmetic  75.8 us (14%)
  starting transfers between devices  48.7 us (9%)
  matrix products  25.2 us (4%)
  between operations  14.3 us (3%)
  local copies, waits for them, and re-layouts  10.4 us (2%)
    reduce_scatter x1, waiting for transfers between devices, on_device(): lax.psum_scatter(lax.dot_general(normalized_rows, grad_hidden, (((0,), (0...  141 us
    psum x1, waiting for transfers between devices, on_device(): grad_w_in = lax.psum(row_share, 'seq')  109 us
    all_gather x1, waiting for transfers between devices, on_device(): full_weight = lax.all_gather(w_in, 'fsdp', axis=0, tiled=True)  67.3 us
    ppermute x35, waiting for transfers between devices, tree_sum(): tree = jax.tree.map(lambda x: x + lax.ppermute(x, axis, route), tree)  66.7 us
    another operation x2, other arithmetic  44.9 us
    ppermute x35, starting transfers between devices, tree_sum(): tree = jax.tree.map(lambda x: x + lax.ppermute(x, axis, route), tree)  44.7 us
    reduce_sum x2, other arithmetic, on_device(): jnp.sum(grad_conv * padded_glu[kernel_len - 1 - offset:kernel_len - 1 - o...  12.6 us
  transfers between devices with their start and end apart: 40, of which 30 were waited for; matrix products, arithmetic and copies ran while one was open for 4% of the time, Pallas kernels for 0%

commit v1 on v0

--- a/solution.py
+++ b/solution.py
@@ -113,7 +113,8 @@
         scatter_dimension=0,
         tiled=True,
     )
-    grad_w_in = lax.psum(row_share, "seq")
+    b_next = lax.all_gather(row_share, axis_name="seq")
+    grad_w_in = jnp.sum(b_next, axis=0)
     return (
         output,
         input_gradient.astype(jnp.bfloat16),

time: 561 us -> 1110 us (1.98)
  waiting for transfers between devices: 387 us -> 929 us
  other arithmetic: 75.8 us -> 94.6 us
    all_gather x0 -> x1, waiting for transfers between devices: none -> 625 us  [on_device(): b_next = lax.all_gather(row_share, axis_name='seq')]
    psum x1 -> x0, waiting for transfers between devices: 109 us -> none  [on_device(): grad_w_in = lax.psum(row_share, 'seq')]
    ppermute x35, waiting for transfers between devices: 66.7 us -> 92.6 us  [tree_sum(): tree = jax.tree.map(lambda x: x + lax.ppermute(x, axis, route), tree)]
    reduce_sum x0 -> x1, other arithmetic: none -> 16.5 us  [on_device(): grad_w_in = jnp.sum(b_next, axis=0)]
  transfers between devices with their start and end apart: 40 -> 40, of which waited for: 30 -> 32; matrix products, arithmetic and copies ran while one was open for 4% -> 2% of each run, Pallas kernels for 0% -> 0%
where the time goes in v1:
time: 1110 us
  waiting for transfers between devices  929 us (84%)
  other arithmetic  94.6 us (9%)
  starting transfers between devices  46.4 us (4%)
  matrix products  24.9 us (2%)
  between operations  14.3 us (1%)
    all_gather x1, waiting for transfers between devices, on_device(): b_next = lax.all_gather(row_share, axis_name='seq')  625 us
    reduce_scatter x1, waiting for transfers between devices, on_device(): lax.psum_scatter(lax.dot_general(normalized_rows, grad_hidden, (((0,), (0...  141 us
    ppermute x35, waiting for transfers between devices, tree_sum(): tree = jax.tree.map(lambda x: x + lax.ppermute(x, axis, route), tree)  92.6 us
    all_gather x1, waiting for transfers between devices, on_device(): full_weight = lax.all_gather(w_in, 'fsdp', axis=0, tiled=True)  67.3 us
    another operation x2, other arithmetic  47.3 us
    ppermute x35, starting transfers between devices, tree_sum(): tree = jax.tree.map(lambda x: x + lax.ppermute(x, axis, route), tree)  42.4 us
  transfers between devices with their start and end apart: 40, of which 32 were waited for; matrix products, arithmetic and copies ran while one was open for 2% of the time, Pallas kernels for 0%

profile of v1, /device:TPU:0, one launch (start us, length us, event | category | flops | bytes accessed | tf_op | source)
XLA Modules:
  0.0 1114.6 jit_solution(17884948880873882363)
XLA Ops:
  9.3 67.3 %all-gather.4.cloned.1.call-done = bf16[1536,3072]{1,0:T(8,128)(2,1)} async-done(((bf16[384,3072]{1,0:T(8,128)(2,1)}), bf16[1536,3072]{1,0:T(8,128)(2,1)}) %all-gather.4.cloned.1.call-update) | async-done | bytes 9437200 | tf_op jit(solution)/shard_map/all_gather | solution.py:42
  76.6 6.5 fusion.114
  83.7 1.5 copy-done
  85.3 2.2 collective-permute-start
  88.7 9.4 fusion.119
  100.0 2.6 collective-permute-start.2
  102.6 1.6 collective-permute-done.2
  104.2 4.1 collective-permute-start.3
  108.3 1.6 collective-permute-done.3
  109.9 2.9 collective-permute-start.4
  112.9 1.6 collective-permute-done.4
  114.5 2.9 collective-permute-start.5
  117.5 1.6 collective-permute-done.5
  120.6 3.6 collective-permute-done.7
  125.4 2.6 collective-permute-done.8
  127.9 2.0 collective-permute-start.9
  129.9 1.6 collective-permute-done.9
  131.6 2.9 collective-permute-start.10
  134.5 1.6 collective-permute-done.10
  136.2 2.5 fusion.116
  140.0 1.9 collective-permute-start.17
  141.9 1.6 collective-permute-done.12
  145.5 1.6 collective-permute-done.13
  147.1 2.0 collective-permute-start.14
  150.8 2.9 collective-permute-start.15
  153.7 1.6 collective-permute-start.20
  155.9 2.3 collective-permute-done.20
  158.3 7.1 multiply_reduce_fusion
  166.8 1.5 collective-permute-start.21
  168.3 1.9 collective-permute-done.21
  170.2 42.9 %multiply_convert_fusion.1 = (bf16[384,1536]{1,0:T(8,128)(2,1)S(1)}, f32[384,1536]{1,0:T(8,128)}) fusion(f32[384,3072]{1,0:T(8,128)} %copy-done, f32[31,1536]{1,0:T(8,128)S(1)} %collective-permute-done.21, f32[384,1536]{1,0:T(8,128)} %copy-done.1, f32[1536]{0:T(1024)S(1)} %get-tuple-element.76, f32[1536]{0:T(1024)S(1)} %get-tuple-element.77, ...), kind=kLoop, calls=%fused_computation.202 | loop fusion | flops 58392576 | bytes 8644608 | tf_op jit(solution)/shard_map/convert
  213.1 4.4 multiply_convert_fusion
  218.5 9.4 fusion.109
  228.2 140.8 %reduce-scatter.2.cloned.1.call-done = f32[384,3072]{1,0:T(8,128)} async-done(((f32[1536,3072]{1,0:T(8,128)}), f32[384,3072]{1,0:T(8,128)}) %reduce-scatter.2.cloned.1.call-update) | async-done | bytes 4718608 | tf_op jit(solution)/shard_map/reduce_scatter | solution.py:105
  369.0 5.4 multiply_reduce_fusion.18
  377.2 6.6 collective-permute-done.23
  383.8 1.5 collective-permute-start.24
  385.4 9.0 fusion.12
  396.2 1.5 collective-permute-start.33
  397.7 1.6 collective-permute-done.28
  401.3 39.4 %collective-permute-done.29 = f32[1536]{0:T(1024)S(1)} collective-permute-done((f32[1536]{0:T(1024)S(1)}, f32[1536]{0:T(1024)S(1)}, u32[]{:S(2)}, u32[]{:S(2)}) %collective-permute-start.29) | collective-permute-done | bytes 6176 | tf_op jit(solution)/shard_map/ppermute | solution.py:22
  441.1 1.7 collective-permute-start.35
  444.8 2.6 collective-permute-start.36
  447.3 3.1 collective-permute-done.25
  450.6 1.8 fusion.11
  453.6 12.4 %collective-permute-done.26 = f32[32,1536]{1,0:T(8,128)S(1)} collective-permute-done((f32[32,1536]{1,0:T(8,128)S(1)}, f32[32,1536]{1,0:T(8,128)S(1)}, u32[]{:S(2)}, u32[]{:S(2)}) %collective-permute-start.26) | collective-permute-done | bytes 196640 | tf_op jit(solution)/shard_map/ppermute | solution.py:22
  466.6 624.9 %all-gather.6.cloned.1.call-done = f32[3072,3072]{1,0:T(8,128)} async-done(((f32[384,3072]{1,0:T(8,128)}), f32[3072,3072]{1,0:T(8,128)}) %all-gather.6.cloned.1.call-update) | async-done | bytes 37748752 | tf_op jit(solution)/shard_map/all_gather | solution.py:116
  1091.6 16.5 %reduce_sum.395 = f32[384,3072]{1,0:T(8,128)} reduce(f32[8,384,3072]{2,1,0:T(8,128)} %bitcast.3, f32[]{:T(128)} %constant.15.clone.1), dimensions={0}, to_apply=%region_9.0 | reduce | flops 8257536 | bytes 42467332 | tf_op jit(solution)/shard_map/reduce_sum | solution.py:117
  (154 shorter events, 27.4 us)
Async XLA Ops:
  7.2 69.4 %copy-start.9 = (f32[1536]{0:T(1024)S(1)}, f32[1536]{0:T(1024)}, u32[]{:S(2)}) copy-start(f32[1536]{0:T(1024)} %param.9) | copy-start | bytes 18436
  7.2 69.4 %copy-start.10 = (f32[1536]{0:T(1024)S(1)}, f32[1536]{0:T(1024)}, u32[]{:S(2)}) copy-start(f32[1536]{0:T(1024)} %param.10) | copy-start | bytes 18436
  7.2 69.4 %all-gather.4.cloned.1.call-start = ((), (), s32[]{:S(2)}) async-start(), calls=%async_computation.1 | async-start | bytes 11796480 | tf_op jit(solution)/shard_map/all_gather | solution.py:42
  7.9 361.0 %reduce-scatter.2.cloned.1.call-start = ((), (), s32[]{:S(2)}) async-start(), calls=%async_computation.2 | async-start | bytes 23592960 | tf_op jit(solution)/shard_map/reduce_scatter | solution.py:105
  85.3 3.1 collective-permute-start
  98.2 38.0 %copy-start.11 = (f32[1536]{0:T(1024)S(1)}, f32[1536]{0:T(1024)}, u32[]{:S(2)}) copy-start(f32[1536]{0:T(1024)} %param.13) | copy-start | bytes 18436
  98.2 38.0 %copy-start.5 = (bf16[384,1536]{1,0:T(8,128)(2,1)S(1)}, bf16[384,1536]{1,0:T(8,128)(2,1)}, u32[]{:S(2)}) copy-start(bf16[384,1536]{1,0:T(8,128)(2,1)} %param.15) | copy-start | bytes 3538948
  98.2 38.0 %copy-start.12 = (f32[1536]{0:T(1024)S(1)}, f32[1536]{0:T(1024)}, u32[]{:S(2)}) copy-start(f32[1536]{0:T(1024)} %param.14) | copy-start | bytes 18436
  98.2 1.8 collective-permute-start.1
  100.0 4.3 collective-permute-start.2
  104.2 5.7 collective-permute-start.3
  109.9 4.6 collective-permute-start.4
  114.5 4.6 collective-permute-start.5
  119.4 1.2 collective-permute-start.6
  120.6 3.7 collective-permute-start.7
  124.3 3.7 collective-permute-start.8
  127.9 3.7 collective-permute-start.9
  131.6 4.5 collective-permute-start.10
  138.6 1.2 collective-permute-start.11
  138.7 1.3 collective-permute-start.16
  139.8 3.7 collective-permute-start.12
  140.0 4.6 collective-permute-start.17
  143.5 3.7 collective-permute-start.13
  144.6 4.6 collective-permute-start.18
  147.1 3.7 collective-permute-start.14
  149.1 4.6 collective-permute-start.19
  150.8 4.5 collective-permute-start.15
  153.7 4.6 collective-permute-start.20
  158.3 7.1 copy-start.13
  166.8 3.3 collective-permute-start.21
  213.0 5.5 copy-start.3
  227.9 863.6 %all-gather.6.cloned.1.call-start = ((), (), s32[]{:S(2)}) async-start(), calls=%async_computation.3 | async-start | bytes 42467328 | tf_op jit(solution)/shard_map/all_gather | solution.py:116
  375.2 1.5 collective-permute-start.22
  376.8 7.0 collective-permute-start.23
  383.8 66.7 %copy-start.4 = (bf16[384,1536]{1,0:T(8,128)(2,1)S(1)}, bf16[384,1536]{1,0:T(8,128)(2,1)}, u32[]{:S(2)}) copy-start(bf16[384,1536]{1,0:T(8,128)(2,1)} %param.8) | copy-start | bytes 3538948
  383.8 59.0 %collective-permute-start.24 = (f32[32,1536]{1,0:T(8,128)S(1)}, f32[32,1536]{1,0:T(8,128)S(1)}, u32[]{:S(2)}, u32[]{:S(2)}) collective-permute-start(f32[32,1536]{1,0:T(8,128)S(1)} %add.429), channel_id=1, source_target_pairs={{0,4},{1,5},{2,6},{3,7},{4,0},{5,1},{6,2},{7,3},{8,12},{9,13},{10,... | collective-permute-start | bytes 589832 | tf_op jit(solution)/shard_map/ppermute | solution.py:22
  394.4 1.2 collective-permute-start.27
  394.5 1.7 collective-permute-start.32
  395.6 3.7 collective-permute-start.28
  396.2 3.7 collective-permute-start.33
  399.3 41.4 %collective-permute-start.29 = (f32[1536]{0:T(1024)S(1)}, f32[1536]{0:T(1024)S(1)}, u32[]{:S(2)}, u32[]{:S(2)}) collective-permute-start(f32[1536]{0:T(1024)S(1)} %add.434), channel_id=1, source_target_pairs={{0,4},{1,5},{2,6},{3,7},{4,0},{5,1},{6,2},{7,3},{8,12},{9,13},{10,... | collective-permute-start | bytes 18440 | tf_op jit(solution)/shard_map/ppermute | solution.py:22
  399.9 41.2 %collective-permute-start.34 = (f32[1536]{0:T(1024)S(1)}, f32[1536]{0:T(1024)S(1)}, u32[]{:S(2)}, u32[]{:S(2)}) collective-permute-start(f32[1536]{0:T(1024)S(1)} %add.439), channel_id=1, source_target_pairs={{0,4},{1,5},{2,6},{3,7},{4,0},{5,1},{6,2},{7,3},{8,12},{9,13},{10,... | collective-permute-start | bytes 18440 | tf_op jit(solution)/shard_map/ppermute | solution.py:22
  440.7 3.7 collective-permute-start.30
  441.1 3.7 collective-permute-start.35
  442.8 7.6 collective-permute-start.25
  444.4 7.9 collective-permute-start.31
  444.8 8.2 collective-permute-start.36
  450.5 15.4 %collective-permute-start.26 = (f32[32,1536]{1,0:T(8,128)S(1)}, f32[32,1536]{1,0:T(8,128)S(1)}, u32[]{:S(2)}, u32[]{:S(2)}) collective-permute-start(f32[32,1536]{1,0:T(8,128)S(1)} %add.431), channel_id=1, source_target_pairs={{0,16},{1,17},{2,18},{3,19},{4,20},{5,21},{6,22},{7,23},{8,24},{9,... | collective-permute-start | bytes 589832 | tf_op jit(solution)/shard_map/ppermute | solution.py:22
  (6 other events, 11.4 us)
Sparse Core Ops, SparseCore 0:
  9.6 66.9 all-gather.3
  228.1 140.8 reduce-scatter.1
  370.6 720.9 all-gather.5
